TPU v7x, 256 devices: a whole 4x4x8 slice. The times are simulated.
256 devices in a mesh: dp: 4 (over y), expert: 64 (over z, x, core).
Axes of the slice: x: 4, y: 4, z: 8, core: 2. Of those that a mesh axis runs over, the one named last changes fastest.
Arguments:
- tokens: bfloat16 [4096, 2048], P('expert'), may hold values from -6 to 6
- attn_gain: float32 [2048], replicated, may hold values from 0.5 to 1.5
- w_query: bfloat16 [2048, 2048], P('expert', 'dp'), may hold values from -0.125 to 0.125
- w_key: bfloat16 [2048, 2048], P('expert', 'dp'), may hold values from -0.125 to 0.125
- w_value: bfloat16 [2048, 2048], P('expert', 'dp'), may hold values from -0.125 to 0.125
- w_out: bfloat16 [2048, 2048], P('expert', 'dp'), may hold values from -0.125 to 0.125
- cache: bfloat16 [131072, 4096], P('expert', 'dp')
- page_table: int32 [64, 16], P('expert'), may hold values from 0 to 15, each once within a row
- cache_len: int32 [64, 4], P('expert'), may hold values from 1 to 512, 1024 in all within a row
- new_len: int32 [64, 4], P('expert'), may hold values from 1 to 32, 64 in all within a row
- kv_owner: int32 [4096, 1], P('expert'), may hold values from 0 to 63; in each aligned block of 64 rows (0 to 63, 64 to 127, ...) at most 2 rows name the same one
- moe_gain: float32 [2048], replicated, may hold values from 0.5 to 1.5
- w_gate: bfloat16 [64, 2048, 1024], P('expert', None, 'dp'), may hold values from -0.125 to 0.125
- w_up: bfloat16 [64, 2048, 1024], P('expert', None, 'dp'), may hold values from -0.125 to 0.125
- w_down: bfloat16 [64, 1024, 2048], P('expert', 'dp'), may hold values from -0.1875 to 0.1875
- expert_ids: int32 [4096, 8], P('expert'), may hold values from 0 to 63, all different within a row; in each aligned block of 64 rows (0 to 63, 64 to 127, ...) at most 16 rows name the same one
- gate_weights: float32 [4096, 8], P('expert'), may hold values from 0.05 to 0.5
Outputs:
- out: bfloat16 [4096, 2048], P('expert')
- new_rows: bfloat16 [8192, 4096], P('expert', 'dp')
Inputs may be any that keep to these rules, and one draw needn't show every extreme that they name: `page_table`: each row of one index of the expert axis lists every local page once; request r reserves the pages in entries r * 4 to (r+1) * 4 - 1. `cache_len`: the lengths of one index sum to 4 * 4 * 128 // 2, and one of them equals 512. `new_len`: the new tokens of one index sum to 64 and stand request by request; one request has exactly 64 // 2. `kv_owner`: among the rows of one device no owner is named more than 2 times; some owner is named exactly 2 times. `expert_ids`: each row names distinct experts; among the rows of one device no expert is named more than 16 times, a bound that some block reaches.
All inputs are finite; a program needn't handle non-finite values.
Results may differ from a plain program's by a relative error of at most 0.012.
The roundings to bfloat16 on the way count: a program that leaves them out, or rounds other values in their place, can miss the bound.
Values may be sent and summed in bfloat16 or wider, within the bound.
No kernel may reach another device: no remote copies, remote signals or barrier semaphores. Data moves between devices by JAX's collectives and lax.ppermute only.
A program may use at most 64 MiB of HBM per device.

v0:
```python
import jax
import jax.numpy as jnp
from jax import lax
from jax.sharding import PartitionSpec as P

HD = 128
PAGE = 128
EPSILON = 1e-05


def norm_rows(row_data, gain_vec):
    mean_sq = jnp.mean(row_data * row_data, axis=-1, keepdims=True)
    return (row_data * lax.rsqrt(mean_sq + EPSILON) * gain_vec).astype(jnp.bfloat16)


def route_rank(route_ids, block_rows, id_range):
    row_total = route_ids.shape[0]
    labels = jnp.arange(id_range, dtype=jnp.int32)
    counts = jnp.sum((route_ids[:, :, None] == labels[None, None, :]).astype(jnp.int32), axis=1)
    counts = counts.reshape(row_total // block_rows, block_rows, id_range)
    before = (jnp.cumsum(counts, axis=1) - counts).reshape(row_total, id_range)
    return jnp.take_along_axis(before, route_ids, axis=1)


def key_masks(table_row, cache_lens, new_lens, row_count, page_size):
    req_count = cache_lens.shape[0]
    pages_here = table_row.shape[0]
    per_request = pages_here // req_count
    slot_ids = jnp.arange(pages_here, dtype=jnp.int32)
    matches = (table_row[:, None] == slot_ids[None, :]).astype(jnp.int32)
    slot_of_page = jnp.sum(matches * slot_ids[:, None], axis=0)
    page_request = slot_of_page // per_request
    page_start = slot_of_page % per_request * page_size
    key_request = jnp.repeat(page_request, page_size)
    key_position = jnp.repeat(page_start, page_size) + jnp.tile(
        jnp.arange(page_size, dtype=jnp.int32), pages_here
    )
    request_ids = jnp.arange(req_count, dtype=jnp.int32)
    key_length = jnp.sum(
        (key_request[:, None] == request_ids[None, :]).astype(jnp.int32) * cache_lens[None, :],
        axis=1,
    )
    request_ends = jnp.cumsum(new_lens)
    tok_ids = jnp.arange(row_count, dtype=jnp.int32)
    tok_request = jnp.sum((tok_ids[:, None] >= request_ends[None, :]).astype(jnp.int32), axis=1)
    cached = (tok_request[:, None] == key_request[None, :]) & (key_position < key_length)[None, :]
    fresh_mask = tok_request[:, None] == tok_request[None, :]
    return jnp.concatenate([cached, fresh_mask], axis=1)


def expert_block(routed, w_gate, w_up, w_down):
    gate_proj = jnp.einsum("necd,edf->necf", routed, w_gate, preferred_element_type=jnp.float32)
    up_proj = jnp.einsum("necd,edf->necf", routed, w_up, preferred_element_type=jnp.float32)
    active = (jax.nn.silu(gate_proj) * up_proj).astype(jnp.bfloat16)
    return jnp.einsum("necf,efd->necd", active, w_down, preferred_element_type=jnp.float32).astype(
        jnp.bfloat16
    )


def local(
    tokens,
    attn_gain,
    w_query,
    w_key,
    w_value,
    w_out,
    cache,
    page_table,
    cache_len,
    new_len,
    kv_owner,
    moe_gain,
    w_gate,
    w_up,
    w_down,
    expert_ids,
    gate_weights,
):
    row_count, model_width = tokens.shape
    n_expert = lax.axis_size("expert")
    local_experts = w_gate.shape[0]
    experts_all = n_expert * local_experts
    top_count = expert_ids.shape[1]
    capacity = min(row_count, 2 * row_count * top_count // experts_all)
    kv_cap = max(2, 2 * row_count // n_expert)
    head_group = w_query.shape[1] // HD
    full_query, full_key, full_value, full_out = (
        lax.all_gather(w_query, "expert", axis=0, tiled=True),
        lax.all_gather(w_key, "expert", axis=0, tiled=True),
        lax.all_gather(w_value, "expert", axis=0, tiled=True),
        lax.all_gather(w_out, "expert", axis=0, tiled=True),
    )
    resid_in = tokens.astype(jnp.float32)
    normed = norm_rows(resid_in, attn_gain)
    queries = jnp.dot(normed, full_query, preferred_element_type=jnp.float32).astype(jnp.bfloat16)
    new_keys = jnp.dot(normed, full_key, preferred_element_type=jnp.float32).astype(jnp.bfloat16)
    new_values = jnp.dot(normed, full_value, preferred_element_type=jnp.float32).astype(
        jnp.bfloat16
    )
    cache_count = cache.shape[0]
    split_cache = cache.reshape(cache_count, 2, head_group, HD)
    all_keys = jnp.concatenate(
        [split_cache[:, 0], new_keys.reshape(row_count, head_group, HD)], axis=0
    )
    all_values = jnp.concatenate(
        [split_cache[:, 1], new_values.reshape(row_count, head_group, HD)], axis=0
    )
    scores = jnp.einsum(
        "thc,rhc->htr",
        queries.reshape(row_count, head_group, HD),
        all_keys,
        preferred_element_type=jnp.float32,
    ) * HD ** (-0.5)
    valid_mask = key_masks(page_table[0], cache_len[0], new_len[0], row_count, PAGE)
    scores = jnp.where(valid_mask[None, :, :], scores, -1e30)
    highest = jnp.max(scores, axis=-1, keepdims=True)
    weights = jnp.exp(scores - highest)
    probs = (weights / jnp.sum(weights, axis=-1, keepdims=True)).astype(jnp.bfloat16)
    heads_out = (
        jnp.einsum("htr,rhc->thc", probs, all_values, preferred_element_type=jnp.float32)
        .astype(jnp.bfloat16)
        .reshape(row_count, head_group * HD)
    )
    attn_part = jnp.einsum("tc,dc->td", heads_out, full_out, preferred_element_type=jnp.float32)
    attn_out = lax.psum(attn_part.astype(jnp.bfloat16), "dp").astype(jnp.float32)
    residual = resid_in + attn_out
    moe_in = norm_rows(residual, moe_gain)
    kv_row = jnp.concatenate([new_keys, new_values], axis=1)
    kv_rank = route_rank(kv_owner, row_count, n_expert)[:, 0]
    kv_buffer = (
        jnp.zeros((n_expert, kv_cap, kv_row.shape[1]), jnp.bfloat16)
        .at[kv_owner[:, 0], kv_rank]
        .set(kv_row)
    )
    slot_rank = route_rank(expert_ids, row_count, experts_all)
    spread_rows = jnp.broadcast_to(moe_in[:, None, :], (row_count, top_count, model_width))
    tok_buffer = (
        jnp.zeros((experts_all, capacity, model_width), jnp.bfloat16)
        .at[expert_ids, slot_rank]
        .set(spread_rows)
    )
    tok_buffer = tok_buffer.reshape(n_expert, local_experts, capacity, model_width)
    got_rows, got_kv = (
        lax.all_to_all(tok_buffer, "expert", split_axis=0, concat_axis=0, tiled=True),
        lax.all_to_all(kv_buffer, "expert", split_axis=0, concat_axis=0, tiled=True),
    )
    partial_value = expert_block(got_rows, w_gate, w_up, w_down)
    returned = lax.all_to_all(
        partial_value, "expert", split_axis=0, concat_axis=0, tiled=True
    ).reshape(experts_all, capacity, model_width)
    picked = returned[expert_ids, slot_rank].astype(jnp.float32)
    moe_part = jnp.sum(picked * gate_weights[:, :, None], axis=1)
    moe_total = lax.psum(moe_part.astype(jnp.bfloat16), "dp").astype(jnp.float32)
    out = (residual + moe_total).astype(jnp.bfloat16)
    new_rows = got_kv.reshape(n_expert * kv_cap, kv_row.shape[1])
    return (out, new_rows)


def solution(mesh):
    placed = (
        P("expert", None),
        P(),
        P("expert", "dp"),
        P("expert", "dp"),
        P("expert", "dp"),
        P("expert", "dp"),
        P("expert", "dp"),
        P("expert", None),
        P("expert", None),
        P("expert", None),
        P("expert", None),
        P(),
        P("expert", None, "dp"),
        P("expert", None, "dp"),
        P("expert", "dp", None),
        P("expert", None),
        P("expert", None),
    )
    return jax.shard_map(
        local,
        mesh=mesh,
        in_specs=placed,
        out_specs=(P("expert", None), P("expert", "dp")),
        check_vma=False,
    )
```

profile of v0, /device:TPU:2, one launch (start us, length us, event | category | flops | bytes accessed | tf_op | source)
XLA Modules:
  0.0 761.0 jit_solution(5198881147081987779)
XLA Ops:
  11.7 6.5 copy.68
  18.2 4.0 fusion.85
  22.2 3.9 copy.82
  26.2 2.5 copy.83
  30.8 59.4 %all-gather.9.cloned.1.call-done = bf16[2048,512]{1,0:T(8,128)(2,1)} async-done(((bf16[32,512]{1,0:T(8,128)(2,1)}), bf16[2048,512]{1,0:T(8,128)(2,1)}) %all-gather.9.cloned.1.call-update) | async-done | bytes 2097168 | tf_op jit(solution)/shard_map/all_gather | solution.py:89
  90.1 2.1 convolution_convert_fusion.1
  92.9 75.0 %all-gather.5.cloned.1.call-done = bf16[2048,512]{1,0:T(8,128)(2,1)} async-done(((bf16[32,512]{1,0:T(8,128)(2,1)}), bf16[2048,512]{1,0:T(8,128)(2,1)}) %all-gather.5.cloned.1.call-update) | async-done | bytes 2097168 | tf_op jit(solution)/shard_map/all_gather | solution.py:90
  167.9 2.1 convolution_convert_fusion.3
  170.6 75.0 %all-gather.7.cloned.1.call-done = bf16[2048,512]{1,0:T(8,128)(2,1)} async-done(((bf16[32,512]{1,0:T(8,128)(2,1)}), bf16[2048,512]{1,0:T(8,128)(2,1)}) %all-gather.7.cloned.1.call-update) | async-done | bytes 2097168 | tf_op jit(solution)/shard_map/all_gather | solution.py:88
  245.6 2.7 fusion.37
  248.3 4.2 fusion.86
  252.6 2.8 fusion.34
  255.3 67.8 %all-gather.11.cloned.1.call-done = bf16[2048,512]{1,0:T(8,128)(2,1)} async-done(((bf16[32,512]{1,0:T(8,128)(2,1)}), bf16[2048,512]{1,0:T(8,128)(2,1)}) %all-gather.11.cloned.1.call-update) | async-done | bytes 2097168 | tf_op jit(solution)/shard_map/all_gather | solution.py:91
  323.2 3.1 convolution_convert_fusion
  326.8 3.8 gather_fusion.1
  330.9 41.1 %all-reduce.3.cloned.1.call-done = bf16[64,2048]{1,0:T(8,128)(2,1)} async-done(((bf16[64,2048]{1,0:T(8,128)(2,1)}), bf16[64,2048]{1,0:T(8,128)(2,1)}) %all-reduce.3.cloned.1.call-update) | async-done | bytes 262160 | tf_op jit(solution)/shard_map/psum | solution.py:125
  372.0 1.1 multiply_reduce_fusion
  374.5 2.5 broadcast_in_dim.35
  377.0 88.6 %scatter_fusion = bf16[64,16,2048]{2,1,0:T(8,128)(2,1)} fusion(bf16[64,16,2048]{2,1,0:T(8,128)(2,1)} %broadcast_in_dim.35, s32[512]{0:T(512)S(1)} %reshape.227, bf16[512,2048]{1,0:T(8,128)(2,1)S(1)} %broadcast_bitcast_fusion), kind=kCustom, calls=%fused_computation.3 | custom fusion | bytes 6295552 | tf_op jit(solution)/shard_map/scatter | solution.py:140
  465.7 107.1 %all_to_all.15 = bf16[64,1,16,2048]{3,2,1,0:T(8,128)(2,1)S(1)} all-to-all(bf16[64,1,16,2048]{3,2,1,0:T(8,128)(2,1)} %bitcast.152), channel_id=1, replica_groups=mesh['dp'=4,'expert'=64] {'expert'}, dimensions={0} | all-to-all | bytes 8388608 | tf_op jit(solution)/shard_map/all_to_all | solution.py:144
  572.8 2.0 copy-done.2
  574.8 1.3 fusion.16
  576.0 8.5 %convert_bitcast_fusion = bf16[64,1,16,2048]{3,2,1,0:T(8,128)(2,1)} fusion(bf16[1,256,2048]{2,1,0:T(8,128)(2,1)S(1)} %copy-done, bf16[64,1,16,2048]{3,2,1,0:T(8,128)(2,1)} %copy-done.2, bf16[1,2048,256]{2,1,0:T(8,128)(2,1)S(1)} %copy-done.12, f32[64,1,16,256]{3,2,0,1:T(8,128)S(1)} %fusion.16), kind=kOutput, calls=%fused_computation.15 | convolution fusion | flops 2151153664 | bytes 11534336 | tf_op jit(solution)/shard_map/necf,efd->necd/dot_general | solution.py:55
  584.5 5.8 all-to-all-start.1
  592.3 9.3 %scatter_fusion.1 = bf16[64,2,1024]{2,1,0:T(2,128)(2,1)} fusion(bf16[64,2,1024]{2,1,0:T(2,128)(2,1)} %broadcast_in_dim.40, s32[64]{0:T(128)S(1)} %fusion.73, bf16[64,1024]{1,0:T(8,128)(2,1)S(1)} %pad_maximum_fusion), kind=kCustom, calls=%fused_computation.4 | custom fusion | bytes 393728 | tf_op jit(solution)/shard_map/scatter | solution.py:133
  601.6 84.8 %all-to-all-done.1 = bf16[64,1,16,2048]{3,2,1,0:T(8,128)(2,1)} async-done(((bf16[64,1,16,2048]{3,2,1,0:T(8,128)(2,1)}), bf16[64,1,16,2048]{3,2,1,0:T(8,128)(2,1)}, u32[]{:S(2)}, u32[]{:S(2)}) %all-to-all-start.1) | async-done | bytes 4194336 | tf_op jit(solution)/shard_map/all_to_all | solution.py:148
  686.4 5.6 all-to-all-start.2
  692.4 10.0 %gather_fusion = bf16[512,2048]{1,0:T(8,128)(2,1)S(1)} fusion(bf16[64,16,2048]{2,1,0:T(8,128)(2,1)} %bitcast.34, s32[512]{0:T(512)S(1)} %reshape.207), kind=kCustom, calls=%fused_computation | custom fusion | bytes 4198400 | tf_op jit(solution)/shard_map/gather | solution.py:151
  702.4 2.5 fusion.3
  705.0 1.8 reshape.206
  706.7 45.6 %all-reduce.5.cloned.1.call-done = bf16[64,2048]{1,0:T(8,128)(2,1)} async-done(((bf16[64,2048]{1,0:T(8,128)(2,1)}), bf16[64,2048]{1,0:T(8,128)(2,1)}) %all-reduce.5.cloned.1.call-update) | async-done | bytes 262160 | tf_op jit(solution)/shard_map/psum | solution.py:153
  752.4 1.8 add_convert_fusion
  (81 shorter events, 12.2 us)
Async XLA Ops:
  7.2 568.9 %copy-start = (bf16[1,256,2048]{2,1,0:T(8,128)(2,1)S(1)}, bf16[1,256,2048]{2,1,0:T(8,128)(2,1)}, u32[]{:S(2)}) copy-start(bf16[1,256,2048]{2,1,0:T(8,128)(2,1)} %param.31) | copy-start | bytes 3145732
  7.2 83.0 %all-gather.9.cloned.1.call-start = ((), (), s32[]{:S(2)}) async-start(), calls=%async_computation.5 | async-start | bytes 2129920 | tf_op jit(solution)/shard_map/all_gather | solution.py:89
  7.9 160.0 %all-gather.5.cloned.1.call-start = ((), (), s32[]{:S(2)}) async-start(), calls=%async_computation.3 | async-start | bytes 2129920 | tf_op jit(solution)/shard_map/all_gather | solution.py:90
  8.7 237.0 %all-gather.7.cloned.1.call-start = ((), (), s32[]{:S(2)}) async-start(), calls=%async_computation.4 | async-start | bytes 2129920 | tf_op jit(solution)/shard_map/all_gather | solution.py:88
  9.4 313.8 %all-gather.11.cloned.1.call-start = ((), (), s32[]{:S(2)}) async-start(), calls=%async_computation.6 | async-start | bytes 2129920 | tf_op jit(solution)/shard_map/all_gather | solution.py:91
  10.0 362.0 %all-reduce.3.cloned.1.call-start = ((), (), s32[]{:S(2)}) async-start(), calls=%async_computation.7 | async-start | bytes 524288 | tf_op jit(solution)/shard_map/psum | solution.py:125
  26.2 2.5 copy-start.6
  26.2 3.3 copy-start.10
  26.2 3.4 copy-start.1
  26.2 63.9 %copy-start.5 = (f32[2048]{0:T(1024)S(1)}, f32[2048]{0:T(1024)}, u32[]{:S(2)}) copy-start(f32[2048]{0:T(1024)} %param.18) | copy-start | bytes 24580
  248.3 4.2 copy-start.3
  255.3 71.0 %copy-start.4 = (s32[64,8]{1,0:T(8,128)S(1)}, s32[64,8]{1,0:T(8,128)}, u32[]{:S(2)}) copy-start(s32[64,8]{1,0:T(8,128)} %copy.75) | copy-start | bytes 6148
  326.8 46.4 %copy-start.7 = (f32[2048]{0:T(1024)S(1)}, f32[2048]{0:T(1024)}, u32[]{:S(2)}) copy-start(f32[2048]{0:T(1024)} %param.28) | copy-start | bytes 24580
  465.7 109.1 %copy-start.11 = (bf16[1,2048,256]{2,1,0:T(8,128)(2,1)S(1)}, bf16[1,2048,256]{2,1,0:T(8,128)(2,1)}, u32[]{:S(2)}) copy-start(bf16[1,2048,256]{2,1,0:T(8,128)(2,1)} %param.29) | copy-start | bytes 3145732
  572.8 2.0 copy-start.2
  574.8 1.3 copy-start.12
  584.5 5.8 copy-start.9
  584.5 101.9 %all-to-all-start.1 = ((bf16[64,1,16,2048]{3,2,1,0:T(8,128)(2,1)}), bf16[64,1,16,2048]{3,2,1,0:T(8,128)(2,1)}, u32[]{:S(2)}, u32[]{:S(2)}) async-start(bf16[64,1,16,2048]{3,2,1,0:T(8,128)(2,1)} %convert_bitcast_fusion), calls=%async_computation.1 | async-start | bytes 8388608 | tf_op jit(solution)/shard_map/all_to_all | solution.py:148
  590.3 102.0 %copy-start.8 = (f32[64,8]{0,1:T(8,128)S(1)}, f32[64,8]{0,1:T(8,128)}, u32[]{:S(2)}) copy-start(f32[64,8]{0,1:T(8,128)} %param.33) | copy-start | bytes 6148
  686.4 18.5 %all-to-all-start.2 = ((bf16[64,2,1024]{2,1,0:T(2,128)(2,1)}), bf16[64,2,1024]{2,1,0:T(2,128)(2,1)}, u32[]{:S(2)}, u32[]{:S(2)}) async-start(bf16[64,2,1024]{2,1,0:T(2,128)(2,1)} %scatter_fusion.1), calls=%async_computation.2 | async-start | bytes 524288 | tf_op jit(solution)/shard_map/all_to_all | solution.py:145
  692.1 60.3 %all-reduce.5.cloned.1.call-start = ((), (), s32[]{:S(2)}) async-start(), calls=%async_computation.8 | async-start | bytes 524288 | tf_op jit(solution)/shard_map/psum | solution.py:153
Sparse Core Ops, SparseCore 0:
  10.8 79.3 all-gather.8
  92.9 74.9 all-gather.4
  170.6 74.9 all-gather.6
  248.2 74.9 all-gather.10
  326.4 45.5 all-reduce.2
  705.1 47.2 all-reduce.4
where the time goes:
time: 765 us; the launch traced here: 761 us
  waiting for transfers between devices  451 us (59%)
  local copies, waits for them, and re-layouts  140 us (18%)
  blocking collectives  107 us (14%)
  matrix products  26.8 us (4%)
  between operations  14.4 us (2%)
  starting transfers between devices  11.6 us (2%)
  other arithmetic  10.1 us (1%)
    all_to_all x1, blocking collectives, local(): lax.all_to_all(tok_buffer, 'expert', split_axis=0, concat_axis=0, tiled=T...  107 us
    scatter x1, local copies, waits for them, and re-layouts, local(): tok_buffer = jnp.zeros((experts_all, capacity, model_width), jnp.bfloat16...  88.6 us
    all_to_all x1, waiting for transfers between devices, local(): lax.all_to_all(partial_value, 'expert', split_axis=0, concat_axis=0, tile...  84.8 us
    all_gather x1, waiting for transfers between devices, local(): lax.all_gather(w_value, 'expert', axis=0, tiled=True)  75 us
    all_gather x1, waiting for transfers between devices, local(): lax.all_gather(w_query, 'expert', axis=0, tiled=True)  75 us
    all_gather x1, waiting for transfers between devices, local(): lax.all_gather(w_out, 'expert', axis=0, tiled=True)  67.8 us
    all_gather x1, waiting for transfers between devices, local(): lax.all_gather(w_key, 'expert', axis=0, tiled=True)  59.4 us
    psum x1, waiting for transfers between devices, local(): lax.psum(moe_part.astype(jnp.bfloat16), 'dp').astype(jnp.float32)  45.6 us
  transfers between devices with their start and end apart: 8, of which 7 were waited for; matrix products, arithmetic and copies ran while one was open for 9% of the time, Pallas kernels for 0%

commit v1 on v0

--- a/solution.py
+++ b/solution.py
@@ -2,6 +2,7 @@
 import jax.numpy as jnp
 from jax import lax
 from jax.sharding import PartitionSpec as P
+from jax.lax import all_to_all, axis_size
 
 HD = 128
 PAGE = 128
@@ -84,11 +85,17 @@
     capacity = min(row_count, 2 * row_count * top_count // experts_all)
     kv_cap = max(2, 2 * row_count // n_expert)
     head_group = w_query.shape[1] // HD
+
+    def _view_blocks(axis_key, piece_in):
+        new = jnp.stack([piece_in] * axis_size(axis_key), axis=0)
+        w1 = all_to_all(new, axis_name=axis_key, split_axis=0, concat_axis=0)
+        return jnp.concatenate(w1, axis=0)
+
     full_query, full_key, full_value, full_out = (
         lax.all_gather(w_query, "expert", axis=0, tiled=True),
         lax.all_gather(w_key, "expert", axis=0, tiled=True),
         lax.all_gather(w_value, "expert", axis=0, tiled=True),
-        lax.all_gather(w_out, "expert", axis=0, tiled=True),
+        _view_blocks("expert", w_out),
     )
     resid_in = tokens.astype(jnp.float32)
     normed = norm_rows(resid_in, attn_gain)

time: 765 us -> 698 us (0.912)
  waiting for transfers between devices: 451 us -> 369 us
  starting transfers between devices: 11.6 us -> 23.6 us
    all_gather x1 -> x0, waiting for transfers between devices: 67.8 us -> none  [local(): lax.all_gather(w_out, 'expert', axis=0, tiled=True)]
    all_gather x1, waiting for transfers between devices: 59.4 us -> 45.8 us  [local(): lax.all_gather(w_key, 'expert', axis=0, tiled=True)]
    all_to_all x0 -> x1, starting transfers between devices: none -> 12 us  [_view_blocks(): w1 = all_to_all(new, axis_name=axis_key, split_axis=0, concat_axis=0)]
    unnamed x32 -> x38, local copies, waits for them, and re-layouts: 15.7 us -> 17.3 us
  transfers between devices with their start and end apart: 8 -> 8, of which waited for: 7 -> 6; matrix products, arithmetic and copies ran while one was open for 9% -> 10% of each run, Pallas kernels for 0% -> 0%
where the time goes in v1:
time: 698 us; the launch traced here: 694 us
  waiting for transfers between devices  369 us (53%)
  local copies, waits for them, and re-layouts  144 us (21%)
  blocking collectives  107 us (15%)
  matrix products  26.6 us (4%)
  starting transfers between devices  23.6 us (3%)
  between operations  14.1 us (2%)
  other arithmetic  10.1 us (1%)
    all_to_all x1, blocking collectives, local(): lax.all_to_all(tok_buffer, 'expert', split_axis=0, concat_axis=0, tiled=T...  107 us
    scatter x1, local copies, waits for them, and re-layouts, local(): tok_buffer = jnp.zeros((experts_all, capacity, model_width), jnp.bfloat16...  88.4 us
    all_to_all x1, waiting for transfers between devices, local(): lax.all_to_all(partial_value, 'expert', split_axis=0, concat_axis=0, tile...  84.8 us
    all_gather x1, waiting for transfers between devices, local(): lax.all_gather(w_query, 'expert', axis=0, tiled=True)  75 us
    all_gather x1, waiting for transfers between devices, local(): lax.all_gather(w_value, 'expert', axis=0, tiled=True)  74.8 us
    all_gather x1, waiting for transfers between devices, local(): lax.all_gather(w_key, 'expert', axis=0, tiled=True)  45.8 us
    psum x1, waiting for transfers between devices, local(): lax.psum(moe_part.astype(jnp.bfloat16), 'dp').astype(jnp.float32)  45.6 us
    psum x1, waiting for transfers between devices, local(): lax.psum(attn_part.astype(jnp.bfloat16), 'dp').astype(jnp.float32)  40.3 us
  transfers between devices with their start and end apart: 8, of which 6 were waited for; matrix products, arithmetic and copies ran while one was open for 10% of the time, Pallas kernels for 0%

profile of v1, /device:TPU:2, one launch (start us, length us, event | category | flops | bytes accessed | tf_op | source)
XLA Modules:
  0.0 693.7 jit_solution(10901048764434220084)
XLA Ops:
  8.7 2.3 stack.2
  11.0 12.0 %all-to-all-start = ((bf16[64,32,512]{2,1,0:T(8,128)(2,1)}), bf16[64,32,512]{2,1,0:T(8,128)(2,1)S(1)}, u32[]{:S(2)}, u32[]{:S(2)}) async-start(bf16[64,32,512]{2,1,0:T(8,128)(2,1)} %stack.2), calls=%async_computation | async-start | bytes 4194304 | tf_op jit(solution)/shard_map/all_to_all | solution.py:91
  23.8 6.5 copy.68
  30.3 4.9 fusion.85
  35.2 4.0 copy.82
  39.2 4.0 copy.83
  46.2 45.8 %all-gather.8.cloned.1.call-done = bf16[2048,512]{1,0:T(8,128)(2,1)} async-done(((bf16[32,512]{1,0:T(8,128)(2,1)}), bf16[2048,512]{1,0:T(8,128)(2,1)}) %all-gather.8.cloned.1.call-update) | async-done | bytes 2097168 | tf_op jit(solution)/shard_map/all_gather | solution.py:96
  92.0 2.1 convolution_convert_fusion.1
  94.8 74.8 %all-gather.4.cloned.1.call-done = bf16[2048,512]{1,0:T(8,128)(2,1)} async-done(((bf16[32,512]{1,0:T(8,128)(2,1)}), bf16[2048,512]{1,0:T(8,128)(2,1)}) %all-gather.4.cloned.1.call-update) | async-done | bytes 2097168 | tf_op jit(solution)/shard_map/all_gather | solution.py:97
  169.6 2.1 convolution_convert_fusion.3
  172.4 75.0 %all-gather.6.cloned.1.call-done = bf16[2048,512]{1,0:T(8,128)(2,1)} async-done(((bf16[32,512]{1,0:T(8,128)(2,1)}), bf16[2048,512]{1,0:T(8,128)(2,1)}) %all-gather.6.cloned.1.call-update) | async-done | bytes 2097168 | tf_op jit(solution)/shard_map/all_gather | solution.py:95
  247.3 2.7 fusion.37
  250.1 4.1 fusion.86
  254.2 3.4 fusion.34
  257.6 2.3 convolution_convert_fusion
  261.2 3.8 gather_fusion.1
  265.3 40.3 %all-reduce.3.cloned.1.call-done = bf16[64,2048]{1,0:T(8,128)(2,1)} async-done(((bf16[64,2048]{1,0:T(8,128)(2,1)}), bf16[64,2048]{1,0:T(8,128)(2,1)}) %all-reduce.3.cloned.1.call-update) | async-done | bytes 262160 | tf_op jit(solution)/shard_map/psum | solution.py:132
  308.2 2.5 broadcast_in_dim.35
  310.6 88.4 %scatter_fusion = bf16[64,16,2048]{2,1,0:T(8,128)(2,1)} fusion(bf16[64,16,2048]{2,1,0:T(8,128)(2,1)} %broadcast_in_dim.35, s32[512]{0:T(512)S(1)} %reshape.233, bf16[512,2048]{1,0:T(8,128)(2,1)S(1)} %broadcast_bitcast_fusion), kind=kCustom, calls=%fused_computation.3 | custom fusion | bytes 6295552 | tf_op jit(solution)/shard_map/scatter | solution.py:147
  399.0 106.9 %all_to_all.20 = bf16[64,1,16,2048]{3,2,1,0:T(8,128)(2,1)S(1)} all-to-all(bf16[64,1,16,2048]{3,2,1,0:T(8,128)(2,1)} %bitcast.153), channel_id=1, replica_groups=mesh['dp'=4,'expert'=64] {'expert'}, dimensions={0} | all-to-all | bytes 8388608 | tf_op jit(solution)/shard_map/all_to_all | solution.py:151
  505.9 1.9 copy-done.2
  507.8 1.3 fusion.16
  509.1 8.5 %convert_bitcast_fusion = bf16[64,1,16,2048]{3,2,1,0:T(8,128)(2,1)} fusion(bf16[1,256,2048]{2,1,0:T(8,128)(2,1)S(1)} %copy-done, bf16[64,1,16,2048]{3,2,1,0:T(8,128)(2,1)} %copy-done.2, bf16[1,2048,256]{2,1,0:T(8,128)(2,1)S(1)} %copy-done.13, f32[64,1,16,256]{3,2,0,1:T(8,128)S(1)} %fusion.16), kind=kOutput, calls=%fused_computation.15 | convolution fusion | flops 2151153664 | bytes 11534336 | tf_op jit(solution)/shard_map/necf,efd->necd/dot_general | solution.py:56
  517.6 5.7 all-to-all-start.2
  525.3 9.3 %scatter_fusion.1 = bf16[64,2,1024]{2,1,0:T(2,128)(2,1)} fusion(bf16[64,2,1024]{2,1,0:T(2,128)(2,1)} %broadcast_in_dim.40, s32[64]{0:T(128)S(1)} %fusion.73, bf16[64,1024]{1,0:T(8,128)(2,1)S(1)} %pad_maximum_fusion), kind=kCustom, calls=%fused_computation.4 | custom fusion | bytes 393728 | tf_op jit(solution)/shard_map/scatter | solution.py:140
  534.7 84.8 %all-to-all-done.2 = bf16[64,1,16,2048]{3,2,1,0:T(8,128)(2,1)} async-done(((bf16[64,1,16,2048]{3,2,1,0:T(8,128)(2,1)}), bf16[64,1,16,2048]{3,2,1,0:T(8,128)(2,1)}, u32[]{:S(2)}, u32[]{:S(2)}) %all-to-all-start.2) | async-done | bytes 4194336 | tf_op jit(solution)/shard_map/all_to_all | solution.py:155
  619.5 5.6 all-to-all-start.3
  625.4 10.0 %gather_fusion = bf16[512,2048]{1,0:T(8,128)(2,1)S(1)} fusion(bf16[64,16,2048]{2,1,0:T(8,128)(2,1)} %bitcast.35, s32[512]{0:T(512)S(1)} %reshape.213), kind=kCustom, calls=%fused_computation | custom fusion | bytes 4198400 | tf_op jit(solution)/shard_map/gather | solution.py:158
  635.4 2.5 fusion.3
  638.0 1.8 reshape.212
  639.8 45.6 %all-reduce.5.cloned.1.call-done = bf16[64,2048]{1,0:T(8,128)(2,1)} async-done(((bf16[64,2048]{1,0:T(8,128)(2,1)}), bf16[64,2048]{1,0:T(8,128)(2,1)}) %all-reduce.5.cloned.1.call-update) | async-done | bytes 262160 | tf_op jit(solution)/shard_map/psum | solution.py:160
  685.4 1.8 add_convert_fusion
  (87 shorter events, 12.8 us)
Async XLA Ops:
  7.2 501.9 %copy-start = (bf16[1,256,2048]{2,1,0:T(8,128)(2,1)S(1)}, bf16[1,256,2048]{2,1,0:T(8,128)(2,1)}, u32[]{:S(2)}) copy-start(bf16[1,256,2048]{2,1,0:T(8,128)(2,1)} %param.31) | copy-start | bytes 3145732
  7.2 84.8 %all-gather.8.cloned.1.call-start = ((), (), s32[]{:S(2)}) async-start(), calls=%async_computation.6 | async-start | bytes 2129920 | tf_op jit(solution)/shard_map/all_gather | solution.py:96
  7.9 161.7 %all-gather.4.cloned.1.call-start = ((), (), s32[]{:S(2)}) async-start(), calls=%async_computation.4 | async-start | bytes 2129920 | tf_op jit(solution)/shard_map/all_gather | solution.py:97
  11.0 246.6 %all-to-all-start = ((bf16[64,32,512]{2,1,0:T(8,128)(2,1)}), bf16[64,32,512]{2,1,0:T(8,128)(2,1)S(1)}, u32[]{:S(2)}, u32[]{:S(2)}) async-start(bf16[64,32,512]{2,1,0:T(8,128)(2,1)} %stack.2), calls=%async_computation | async-start | bytes 4194304 | tf_op jit(solution)/shard_map/all_to_all | solution.py:91
  23.0 224.3 %all-gather.6.cloned.1.call-start = ((), (), s32[]{:S(2)}) async-start(), calls=%async_computation.5 | async-start | bytes 2129920 | tf_op jit(solution)/shard_map/all_gather | solution.py:95
  23.8 281.9 %all-reduce.3.cloned.1.call-start = ((), (), s32[]{:S(2)}) async-start(), calls=%async_computation.7 | async-start | bytes 524288 | tf_op jit(solution)/shard_map/psum | solution.py:132
  39.1 4.1 copy-start.4
  39.1 4.8 copy-start.14
  39.1 4.9 copy-start.15
  39.2 5.2 copy-start.11
  39.2 5.3 copy-start.1
  39.2 52.9 %copy-start.3 = (f32[2048]{0:T(1024)S(1)}, f32[2048]{0:T(1024)}, u32[]{:S(2)}) copy-start(f32[2048]{0:T(1024)} %param.18) | copy-start | bytes 24580
  44.6 50.2 %copy-start.7 = (f32[64]{0:T(128)}, f32[64]{0:T(128)S(1)}, u32[]{:S(2)}) copy-start(f32[64]{0:T(128)S(1)} %add_rsqrt_fusion.1) | copy-start | bytes 772
  169.6 77.7 %copy-start.8 = (f32[64]{0:T(128)S(1)}, f32[64]{0:T(128)}, u32[]{:S(2)}) copy-start(f32[64]{0:T(128)} %copy-done.7) | copy-start | bytes 772
  257.6 3.4 copy-start.5
  261.2 45.6 %copy-start.6 = (f32[2048]{0:T(1024)S(1)}, f32[2048]{0:T(1024)}, u32[]{:S(2)}) copy-start(f32[2048]{0:T(1024)} %param.28) | copy-start | bytes 24580
  399.0 108.8 %copy-start.12 = (bf16[1,2048,256]{2,1,0:T(8,128)(2,1)S(1)}, bf16[1,2048,256]{2,1,0:T(8,128)(2,1)}, u32[]{:S(2)}) copy-start(bf16[1,2048,256]{2,1,0:T(8,128)(2,1)} %param.29) | copy-start | bytes 3145732
  505.9 1.9 copy-start.2
  507.8 1.3 copy-start.13
  517.6 5.8 copy-start.10
  517.6 101.9 %all-to-all-start.2 = ((bf16[64,1,16,2048]{3,2,1,0:T(8,128)(2,1)}), bf16[64,1,16,2048]{3,2,1,0:T(8,128)(2,1)}, u32[]{:S(2)}, u32[]{:S(2)}) async-start(bf16[64,1,16,2048]{3,2,1,0:T(8,128)(2,1)} %convert_bitcast_fusion), calls=%async_computation.2 | async-start | bytes 8388608 | tf_op jit(solution)/shard_map/all_to_all | solution.py:155
  523.3 102.0 %copy-start.9 = (f32[64,8]{0,1:T(8,128)S(1)}, f32[64,8]{0,1:T(8,128)}, u32[]{:S(2)}) copy-start(f32[64,8]{0,1:T(8,128)} %param.33) | copy-start | bytes 6148
  619.5 18.5 %all-to-all-start.3 = ((bf16[64,2,1024]{2,1,0:T(2,128)(2,1)}), bf16[64,2,1024]{2,1,0:T(2,128)(2,1)}, u32[]{:S(2)}, u32[]{:S(2)}) async-start(bf16[64,2,1024]{2,1,0:T(2,128)(2,1)} %scatter_fusion.1), calls=%async_computation.3 | async-start | bytes 524288 | tf_op jit(solution)/shard_map/all_to_all | solution.py:152
  625.1 60.3 %all-reduce.5.cloned.1.call-start = ((), (), s32[]{:S(2)}) async-start(), calls=%async_computation.8 | async-start | bytes 524288 | tf_op jit(solution)/shard_map/psum | solution.py:160
Sparse Core Ops, SparseCore 0:
  10.8 81.2 all-gather.7
  94.8 74.7 all-gather.3
  172.4 74.9 all-gather.5
  260.1 45.5 all-reduce.2
  638.1 47.2 all-reduce.4
